TPU v7x, 128 devices: a whole 4x4x4 slice. The times are simulated.
128 devices in a mesh: item: 4 (over y_hi, core), row: 8 (over y_lo, x), col: 4 (over z).
Axes of the slice: x: 4, y: 4 (y_hi: 2, y_lo: 2; y = y_hi * 2 + y_lo), z: 4, core: 2. Of those that a mesh axis runs over, the one named last changes fastest.
Arguments:
- latents: bfloat16 [64, 64, 4, 2432], P('row', 'col', 'item'), may hold values from -6 to 6
- prompt_tokens: bfloat16 [160, 4, 2432], P('row', 'item'), may hold values from -6 to 6
- text_count: int32 [4], P('item'), may hold values from 1 to 160, as said below
- step_index: int32 [4], P('item'), may hold values from 0 to 27
- step_table: float32 [28, 6, 2432], replicated, may hold values from -3 to 3
- item_mod: float32 [4, 6, 2432], P('item'), may hold values from -3 to 3
- w_qkv: bfloat16 [2432, 3, 1536], P(None, None, 'col'), may hold values from -1 to 1
- w_kv_text: bfloat16 [2432, 2, 1536], P(None, None, 'col'), may hold values from -0.125 to 0.125
- q_gain: float32 [64], replicated, may hold values from 0.5 to 6.5
- k_gain: float32 [64], replicated, may hold values from 0.5 to 6.5
- w_out: bfloat16 [1536, 2432], P('col'), may hold values from -0.15625 to 0.15625
- w_up: bfloat16 [2432, 9728], P(None, ('item', 'col')), may hold values from -0.125 to 0.125
- w_down: bfloat16 [9728, 2432], P(('item', 'col')), may hold values from -0.0625 to 0.0625
Outputs:
- updated: bfloat16 [64, 64, 4, 2432], P('row', 'col', 'item')
Inputs may be any that keep to these rules, and one draw needn't show every extreme that they name: `text_count`: some item has all 160 text tokens live.
All inputs are finite; a program needn't handle non-finite values.
Results may differ from a plain program's by a relative error of at most 0.022.
The roundings to bfloat16 on the way count: a program that leaves them out, or rounds other values in their place, can miss the bound.
Values may be sent and summed in bfloat16 or wider, within the bound.
No kernel may reach another device: no remote copies, remote signals or barrier semaphores. Data moves between devices by JAX's collectives and lax.ppermute only.
A program may use at most 192 MiB of HBM per device.

v0:
```python
import jax
import jax.numpy as jnp
from jax import lax
from jax.sharding import PartitionSpec as P

epsilon = 1e-06


def layer_norm(values):
    values = values.astype(jnp.float32)
    center = values - jnp.mean(values, axis=-1, keepdims=True)
    variance = jnp.mean(center * center, axis=-1, keepdims=True)
    return center * lax.rsqrt(variance + epsilon)


def rms_heads(values, gain):
    return values * lax.rsqrt(jnp.mean(values * values, axis=-1, keepdims=True) + epsilon) * gain


def local(
    latents,
    prompt_tokens,
    text_count,
    step_index,
    step_table,
    item_mod,
    w_qkv,
    w_kv_text,
    q_gain,
    k_gain,
    w_out,
    w_up,
    w_down,
):
    grid_rows, grid_cols, local_items, model_width = latents.shape
    own_rows = grid_rows * grid_cols
    tokens = latents.reshape(own_rows, local_items, model_width)
    wide_up, wide_down = (w_up, w_down)
    chosen = (
        step_index[:, None] == jnp.arange(step_table.shape[0], dtype=jnp.int32)[None, :]
    ).astype(jnp.float32)
    modulation = (
        jnp.einsum("is,sjd->ijd", chosen, step_table, precision=lax.Precision.HIGHEST) + item_mod
    )
    strip_rows = lax.all_gather(tokens, "col", axis=0, tiled=True)
    strip_len = strip_rows.shape[0]
    normed_one = (layer_norm(strip_rows) * (1.0 + modulation[:, 1]) + modulation[:, 0]).astype(
        jnp.bfloat16
    )
    projected = jnp.einsum("sid,dce->csie", normed_one, w_qkv, preferred_element_type=jnp.float32)
    head_cols = w_qkv.shape[2]
    local_heads = head_cols // 64
    query = rms_heads(projected[0].reshape(strip_len, local_items, local_heads, 64), q_gain).astype(
        jnp.bfloat16
    )
    key_img = (
        rms_heads(projected[1].reshape(strip_len, local_items, local_heads, 64), k_gain)
        .astype(jnp.bfloat16)
        .reshape(strip_len, local_items, head_cols)
    )
    value_img = projected[2].astype(jnp.bfloat16)
    text_len = prompt_tokens.shape[0]
    text_normed = layer_norm(prompt_tokens).astype(jnp.bfloat16)
    text_proj = jnp.einsum(
        "tid,dce->ctie", text_normed, w_kv_text, preferred_element_type=jnp.float32
    )
    text_key = (
        rms_heads(text_proj[0].reshape(text_len, local_items, local_heads, 64), k_gain)
        .astype(jnp.bfloat16)
        .reshape(text_len, local_items, head_cols)
    )
    text_value = text_proj[1].astype(jnp.bfloat16)
    position = lax.axis_index("row") * text_len + jnp.arange(text_len, dtype=jnp.int32)
    text_bias = jnp.where(position[:, None] < text_count[None, :], 0.0, -jnp.inf).astype(
        jnp.float32
    )
    run_max = jnp.full((local_items, local_heads, strip_len), -jnp.inf, jnp.float32)
    run_sum = jnp.zeros((local_items, local_heads, strip_len), jnp.float32)
    accum = jnp.zeros((local_items, local_heads, strip_len, 64), jnp.float32)
    key_piece = lax.all_gather(key_img, "row", axis=0, tiled=True)
    value_piece = lax.all_gather(value_img, "row", axis=0, tiled=True)
    tkey_piece = lax.all_gather(text_key, "row", axis=0, tiled=True)
    tvalue_piece = lax.all_gather(text_value, "row", axis=0, tiled=True)
    bias_piece = lax.all_gather(text_bias.astype(jnp.bfloat16), "row", axis=0, tiled=True).astype(
        jnp.float32
    )
    key_piece = key_piece.reshape(key_piece.shape[0], local_items, local_heads, 64)
    value_piece = value_piece.reshape(value_piece.shape[0], local_items, local_heads, 64)
    tkey_piece = tkey_piece.reshape(tkey_piece.shape[0], local_items, local_heads, 64)
    tvalue_piece = tvalue_piece.reshape(tvalue_piece.shape[0], local_items, local_heads, 64)
    score_img = (
        jnp.einsum("sihd,kihd->ihsk", query, key_piece, preferred_element_type=jnp.float32) * 0.125
    )
    score_txt = (
        jnp.einsum("sihd,kihd->ihsk", query, tkey_piece, preferred_element_type=jnp.float32) * 0.125
    )
    score_txt = score_txt + jnp.transpose(bias_piece)[:, None, None, :]
    new_max = jnp.maximum(
        run_max, jnp.maximum(jnp.max(score_img, axis=-1), jnp.max(score_txt, axis=-1))
    )
    rescale = jnp.exp(run_max - new_max)
    prob_img = jnp.exp(score_img - new_max[..., None])
    prob_txt = jnp.exp(score_txt - new_max[..., None])
    run_sum = run_sum * rescale + jnp.sum(prob_img, axis=-1) + jnp.sum(prob_txt, axis=-1)
    accum = accum * rescale[..., None]
    accum = accum + jnp.einsum(
        "ihsk,kihd->ihsd",
        prob_img.astype(jnp.bfloat16),
        value_piece,
        preferred_element_type=jnp.float32,
    )
    accum = accum + jnp.einsum(
        "ihsk,kihd->ihsd",
        prob_txt.astype(jnp.bfloat16),
        tvalue_piece,
        preferred_element_type=jnp.float32,
    )
    run_max, run_sum, accum = (new_max, run_sum, accum)
    heads_out = (accum / run_sum[..., None]).astype(jnp.bfloat16)
    attended = jnp.transpose(heads_out, (2, 0, 1, 3)).reshape(strip_len, local_items, head_cols)
    block_rows = attended
    attn_out = lax.psum_scatter(
        jnp.einsum("sie,ed->sid", block_rows, w_out, preferred_element_type=jnp.float32).astype(
            jnp.bfloat16
        ),
        "col",
        scatter_dimension=0,
        tiled=True,
    ).astype(jnp.float32)
    residual = (tokens.astype(jnp.float32) + modulation[:, 2] * attn_out).astype(jnp.bfloat16)
    normed_two = (layer_norm(residual) * (1.0 + modulation[:, 4]) + modulation[:, 3]).astype(
        jnp.bfloat16
    )
    residual, flat_rows = (residual, normed_two.reshape(own_rows * local_items, model_width))
    hidden = jax.nn.gelu(
        jnp.dot(
            lax.all_gather(flat_rows, ("item", "col"), axis=0, tiled=True),
            wide_up,
            preferred_element_type=jnp.float32,
        ),
        approximate=True,
    ).astype(jnp.bfloat16)
    block_rows = hidden
    mlp_sum = lax.psum_scatter(
        jnp.dot(block_rows, wide_down, preferred_element_type=jnp.float32).astype(jnp.bfloat16),
        ("item", "col"),
        scatter_dimension=0,
        tiled=True,
    ).astype(jnp.float32)
    mlp_sum = mlp_sum.reshape(own_rows, local_items, model_width)
    updated = (residual.astype(jnp.float32) + modulation[:, 5] * mlp_sum).astype(jnp.bfloat16)
    return updated.reshape(grid_rows, grid_cols, local_items, model_width)


def solution(mesh):
    placed = (
        P("row", "col", "item", None),
        P("row", "item", None),
        P("item"),
        P("item"),
        P(),
        P("item", None, None),
        P(None, None, "col"),
        P(None, None, "col"),
        P(),
        P(),
        P("col", None),
        P(None, ("item", "col")),
        P(("item", "col"), None),
    )
    return jax.shard_map(
        local, mesh=mesh, in_specs=placed, out_specs=P("row", "col", "item", None), check_vma=False
    )
```

profile of v0, /device:TPU:1, one launch (start us, length us, event | category | flops | bytes accessed | tf_op | source)
XLA Modules:
  0.0 471.7 jit_solution(10957942517682658492)
XLA Ops:
  6.5 0.7 all-gather.8.cloned.1.call-update
  8.1 2.2 fusion.77
  10.3 0.7 mul.292
  11.1 0.9 reshape_add_fusion
  11.9 0.2 slice_reduce_fusion.1
  12.1 34.5 %all-gather.8.cloned.1.call-done = bf16[512,1,2432]{2,0,1:T(8,128)(2,1)} async-done(((bf16[128,1,2432]{2,0,1:T(8,128)(2,1)}), bf16[512,1,2432]{2,0,1:T(8,128)(2,1)}) %all-gather.8.cloned.1.call-update) | async-done | bytes 2490384 | tf_op jit(solution)/shard_map/all_gather | solution.py:45
  46.6 2.3 convert_reduce_fusion
  48.9 0.2 copy-done.1
  49.0 0.8 fusion.8
  49.8 6.1 %fusion.39 = f32[3,512,1,384]{1,3,0,2:T(8,128)S(1)} fusion(bf16[2432,3,384]{2,0,1:T(8,128)(2,1)} %param.19, bf16[512,1,2432]{2,0,1:T(8,128)(2,1)S(1)} %copy-done.1, f32[2432]{0:T(1024)S(1)} %get-tuple-element.8, f32[2432]{0:T(1024)S(1)} %get-tuple-element.9, f32[512]{0:T(512)S(1)} %add_rsqrt_fusion.3, f32[512]{0:T(512)S(1)} %broadcast_multiply_fusion), kind=kOutput, calls=%fused_computation.45 | convolution fusion | flops 2876375040 | bytes 10476544 | tf_op jit(solution)/shard_map/sid,dce->csie/dot_general | solution.py:50
  56.0 1.4 copy-done.4
  57.4 1.6 slice_multiply_fusion.2
  59.0 1.2 reduce_sum.102
  60.3 2.1 fusion.64
  62.5 0.1 convert_reduce_fusion.2
  62.6 0.2 fusion.67
  62.9 2.7 fusion.56
  65.7 0.1 reduce_sum.105
  65.9 0.1 mul.304
  66.0 25.3 %all_gather.23 = bf16[160,1,384]{2,1,0:T(2,128)(2,1)S(1)} all-gather(bf16[20,1,384]{2,1,0:T(2,128)(2,1)S(1)} %copy.26), channel_id=1, replica_groups=mesh['item'=4,'row'=8,'col'=4] {'row'}, dimensions={0}, use_global_device_ids=true | all-gather | bytes 138240 | tf_op jit(solution)/shard_map/all_gather | solution.py:82
  91.3 0.2 copy.27
  92.2 0.6 dynamic-slice
  93.4 0.2 dynamic-update-slice
  93.6 16.2 %all-reduce = bf16[160]{0:T(256)(128)(2,1)S(1)} all-reduce(bf16[160]{0:T(256)(128)(2,1)S(1)} %dynamic-update-slice), channel_id=1, replica_groups=mesh['item'=4,'row'=8,'col'=4] {'row'}, use_global_device_ids=true, to_apply=%add | all-reduce | flops 160 | bytes 640
  109.8 22.0 %all-gather.1 = bf16[1,160,1,384]{3,2,0,1:T(2,128)(2,1)S(1)} all-gather(bf16[1,20,1,384]{3,2,0,1:T(2,128)(2,1)S(1)} %copy.28), channel_id=3, replica_groups=mesh['item'=4,'row'=8,'col'=4] {'row'}, dimensions={1}, use_global_device_ids=true | all-gather | bytes 138240 | tf_op jit(solution)/shard_map/all_gather | solution.py:83
  131.8 0.9 copy.29
  132.7 1.9 slice.74
  134.7 1.2 reduce_sum.101
  135.9 0.2 reduce-scatter.3.cloned.1.call-start
  136.2 2.9 fusion.38
  139.1 21.7 %multiply_reduce_fusion = (f32[6,512]{1,0:T(8,128)S(1)}, f32[6,512,4096]{2,1,0:T(8,128)}) fusion(bf16[4096,6,64]{0,2,1:T(8,128)(2,1)} %bitcast.91, f32[512,6,64]{0,2,1:T(8,128)} %bitcast.90, f32[64]{0:T(128)S(1)} %copy-done.8, f32[512,6]{0,1:T(8,128)S(1)} %add_rsqrt_fusion.1), kind=kOutput, calls=%fused_computation.1 | convolution fusion | flops 1636365312 | bytes 54288640 | tf_op jit(solution)/shard_map/sihd,kihd->ihsk/dot_general | solution.py:92
  160.7 2.1 fusion.42
  162.8 20.8 %fusion = f32[6,512]{1,0:T(8,128)S(1)} fusion(f32[6,512,4096]{2,1,0:T(8,128)} %get-tuple-element.19, f32[6,512]{1,0:T(8,128)S(1)} %get-tuple-element.14), kind=kLoop, calls=%fused_computation.2 | loop fusion | flops 37745664 | bytes 50356224 | tf_op jit(solution)/shard_map/reduce_sum | solution.py:104
  183.6 4.3 all-gather.12.cloned.1.call-done
  187.9 19.8 %fusion.47 = f32[6,512,64]{1,2,0:T(8,128)S(1)} fusion(bf16[4096,6,64]{0,2,1:T(8,128)(2,1)} %bitcast.95, f32[6,512,4096]{2,1,0:T(8,128)} %get-tuple-element.19, f32[6,512]{1,0:T(8,128)S(1)} %get-tuple-element.14, f32[6,512]{1,0:T(8,128)S(1)} %get-tuple-element.13), kind=kOutput, calls=%fused_computation.52 | convolution fusion | flops 1648558080 | bytes 54288384 | tf_op jit(solution)/shard_map/ihsk,kihd->ihsd/dot_general | solution.py:106
  207.7 0.6 fusion.50
  208.4 0.8 copy-done.5
  209.2 3.0 fusion.20
  212.3 39.9 %reduce-scatter.3.cloned.1.call-done = bf16[128,1,2432]{2,0,1:T(8,128)(2,1)} async-done(((bf16[512,1,2432]{2,0,1:T(8,128)(2,1)}), bf16[128,1,2432]{2,0,1:T(8,128)(2,1)}) %reduce-scatter.3.cloned.1.call-update) | async-done | bytes 622608 | tf_op jit(solution)/shard_map/reduce_scatter | solution.py:122
  252.2 1.6 convert_reduce_fusion.1
  253.8 0.3 fusion.51
  254.1 0.5 copy-done.2
  254.6 1.3 fusion.54
  255.9 0.3 reduce-scatter.5.cloned.1.call-start
  256.2 79.7 %all-gather.14.cloned.1.call-done = bf16[2048,1,2432]{2,0,1:T(8,128)(2,1)} async-done(((bf16[128,1,2432]{2,0,1:T(8,128)(2,1)}), bf16[2048,1,2432]{2,0,1:T(8,128)(2,1)}) %all-gather.14.cloned.1.call-update) | async-done | bytes 9961488 | tf_op jit(solution)/shard_map/all_gather | solution.py:137
  335.8 20.5 %convolution_convert_fusion = bf16[2048,2432]{1,0:T(8,128)(2,1)} fusion(bf16[608,2432]{1,0:T(8,128)(2,1)S(1)} %copy-done, bf16[2432,608]{0,1:T(8,128)(2,1)} %param.24, bf16[2048,1,2432]{2,0,1:T(8,128)(2,1)} %all-gather.14.cloned.1.call-done), kind=kOutput, calls=%fused_computation.5 | convolution fusion | flops 12129337344 | bytes 25837568 | tf_op jit(solution)/shard_map/dot_general | solution.py:145
  356.3 106.2 %reduce-scatter.5.cloned.1.call-done = bf16[128,2432]{1,0:T(8,128)(2,1)} async-done(((bf16[2048,2432]{1,0:T(8,128)(2,1)}), bf16[128,2432]{1,0:T(8,128)(2,1)}) %reduce-scatter.5.cloned.1.call-update) | async-done | bytes 622608 | tf_op jit(solution)/shard_map/reduce_scatter | solution.py:144
  462.6 2.3 fusion.55
  (50 shorter events, 0.8 us)
Async XLA Ops:
  6.5 329.3 %copy-start = (bf16[608,2432]{1,0:T(8,128)(2,1)S(1)}, bf16[608,2432]{1,0:T(8,128)(2,1)}, u32[]{:S(2)}) copy-start(bf16[608,2432]{1,0:T(8,128)(2,1)} %param.25) | copy-start | bytes 8871940
  6.5 40.1 %all-gather.8.cloned.1.call-start = ((), (), s32[]{:S(2)}) async-start(), calls=%async_computation.2 | async-start | bytes 3112960 | tf_op jit(solution)/shard_map/all_gather | solution.py:45
  7.3 131.8 %all-gather.10.cloned.1.call-start = ((), (), s32[]{:S(2)}) async-start(), calls=%async_computation.3 | async-start | bytes 3538944 | tf_op jit(solution)/shard_map/all_gather | solution.py:80
  46.6 2.5 copy-start.1
  56.0 1.4 copy-start.4
  59.0 3.5 copy-start.6
  62.4 29.8 %copy-start.9 = (u32[128]{0:T(128)S(1)}, u32[128]{0:T(128)}, u32[]{:S(2)}) copy-start(u32[128]{0:T(128)} %constant.56) | copy-start | bytes 1540
  62.4 125.4 %all-gather.12.cloned.1.call-start = ((), (), s32[]{:S(2)}) async-start(), calls=%async_computation.6 | async-start | bytes 3538944 | tf_op jit(solution)/shard_map/all_gather | solution.py:81
  65.6 70.6 %copy-start.8 = (f32[64]{0:T(128)S(1)}, f32[64]{0:T(128)}, u32[]{:S(2)}) copy-start(f32[64]{0:T(128)} %param.21) | copy-start | bytes 772
  135.9 116.3 %reduce-scatter.3.cloned.1.call-start = ((), (), s32[]{:S(2)}) async-start(), calls=%async_computation.4 | async-start | bytes 3112960 | tf_op jit(solution)/shard_map/reduce_scatter | solution.py:122
  187.8 19.9 %copy-start.3 = (f32[6,512,160]{1,2,0:T(8,128)S(1)}, f32[6,512,160]{1,2,0:T(8,128)}, u32[]{:S(2)}) copy-start(f32[6,512,160]{1,2,0:T(8,128)} %get-tuple-element.21) | copy-start | bytes 5898244
  187.8 19.9 %copy-start.7 = (bf16[1,160,1,384]{1,3,2,0:T(8,128)(2,1)S(1)}, bf16[1,160,1,384]{1,3,2,0:T(8,128)(2,1)}, u32[]{:S(2)}) copy-start(bf16[1,160,1,384]{1,3,2,0:T(8,128)(2,1)} %copy.29) | copy-start | bytes 368644
  207.7 1.5 copy-start.5
  212.2 123.6 %all-gather.14.cloned.1.call-start = ((), (), s32[]{:S(2)}) async-start(), calls=%async_computation.7 | async-start | bytes 10584064 | tf_op jit(solution)/shard_map/all_gather | solution.py:137
  253.7 0.8 copy-start.2
  255.9 206.7 %reduce-scatter.5.cloned.1.call-start = ((), (), s32[]{:S(2)}) async-start(), calls=%async_computation.5 | async-start | bytes 10584064 | tf_op jit(solution)/shard_map/reduce_scatter | solution.py:144
Sparse Core Ops, SparseCore 0:
  9.0 37.5 all-gather.7
  62.5 44.3 all-gather.9
  136.0 51.7 all-gather.11
  212.3 39.7 reduce-scatter.2
  256.0 79.7 all-gather.13
  356.5 106.0 reduce-scatter.4
where the time goes:
time: 473 us; the launch traced here: 472 us
  waiting for transfers between devices  265 us (56%)
  matrix products  79.6 us (17%)
  blocking collectives  63.5 us (13%)
  other arithmetic  39 us (8%)
  between operations  15.7 us (3%)
  local copies, waits for them, and re-layouts  7.92 us (2%)
    reduce_scatter x1, waiting for transfers between devices, local(): lax.psum_scatter(jnp.dot(block_rows, wide_down, preferred_element_type=jn...  106 us
    all_gather x1, waiting for transfers between devices, local(): lax.all_gather(flat_rows, ('item', 'col'), axis=0, tiled=True)  79.7 us
    reduce_scatter x1, waiting for transfers between devices, local(): lax.psum_scatter(jnp.einsum('sie,ed->sid', block_rows, w_out, preferred_e...  39.9 us
    all_gather x1, waiting for transfers between devices, local(): strip_rows = lax.all_gather(tokens, 'col', axis=0, tiled=True)  34.5 us
    all_gather x1, blocking collectives, local(): tkey_piece = lax.all_gather(text_key, 'row', axis=0, tiled=True)  25.3 us
    all_gather x1, blocking collectives, local(): tvalue_piece = lax.all_gather(text_value, 'row', axis=0, tiled=True)  22 us
    dot_general x1, matrix products, local(): jnp.einsum('sihd,kihd->ihsk', query, key_piece, preferred_element_type=jn...  21.7 us
    reduce_sum x1, other arithmetic, local(): jnp.sum(prob_img, axis=-1)  20.8 us
  transfers between devices with their start and end apart: 6, of which 5 were waited for; matrix products, arithmetic and copies ran while one was open for 13% of the time, Pallas kernels for 0%

commit v1 on v0

--- a/solution.py
+++ b/solution.py
@@ -4,6 +4,11 @@
 from jax.sharding import PartitionSpec as P
 
 epsilon = 1e-06
+
+
+def tiled_gather(x, axis, dim):
+    copies = jnp.concatenate([x] * lax.axis_size(axis), axis=dim)
+    return lax.all_to_all(copies, axis, dim, dim, tiled=True)
 
 
 def layer_norm(values):
@@ -42,7 +47,7 @@
     modulation = (
         jnp.einsum("is,sjd->ijd", chosen, step_table, precision=lax.Precision.HIGHEST) + item_mod
     )
-    strip_rows = lax.all_gather(tokens, "col", axis=0, tiled=True)
+    strip_rows = tiled_gather(tokens, "col", 0)
     strip_len = strip_rows.shape[0]
     normed_one = (layer_norm(strip_rows) * (1.0 + modulation[:, 1]) + modulation[:, 0]).astype(
         jnp.bfloat16

time: 473 us -> 489 us (1.034)
  local copies, waits for them, and re-layouts: 7.92 us -> 18.2 us
  other arithmetic: 39 us -> 47.3 us
  waiting for transfers between devices: 265 us -> 257 us
  starting transfers between devices: 0.61 us -> 6.56 us
    all_gather x1 -> x0, waiting for transfers between devices: 34.5 us -> none  [local(): strip_rows = lax.all_gather(tokens, 'col', axis=0, tiled=True)]
    all_to_all x0 -> x1, waiting for transfers between devices: none -> 26.8 us  [tiled_gather(): return lax.all_to_all(copies, axis, dim, dim, tiled=True)]
    unnamed x23 -> x29, local copies, waits for them, and re-layouts: 3.77 us -> 14.2 us
    concatenate x0 -> x2, other arithmetic: none -> 8.51 us  [tiled_gather(): copies = jnp.concatenate([x] * lax.axis_size(axis), axis=dim)]
    all_to_all x0 -> x1, starting transfers between devices: none -> 5.99 us  [tiled_gather(): return lax.all_to_all(copies, axis, dim, dim, tiled=True)]
  transfers between devices with their start and end apart: 6 -> 6, of which waited for: 5 -> 5; matrix products, arithmetic and copies ran while one was open for 13% -> 12% of each run, Pallas kernels for 0% -> 0%
where the time goes in v1:
time: 489 us; the launch traced here: 488 us
  waiting for transfers between devices  257 us (53%)
  matrix products  79.6 us (16%)
  blocking collectives  63.8 us (13%)
  other arithmetic  47.3 us (10%)
  local copies, waits for them, and re-layouts  18.2 us (4%)
  between operations  15.3 us (3%)
  starting transfers between devices  6.56 us (1%)
    reduce_scatter x1, waiting for transfers between devices, local(): lax.psum_scatter(jnp.dot(block_rows, wide_down, preferred_element_type=jn...  106 us
    all_gather x1, waiting for transfers between devices, local(): lax.all_gather(flat_rows, ('item', 'col'), axis=0, tiled=True)  79.7 us
    reduce_scatter x1, waiting for transfers between devices, local(): lax.psum_scatter(jnp.einsum('sie,ed->sid', block_rows, w_out, preferred_e...  39.8 us
    all_to_all x1, waiting for transfers between devices, tiled_gather(): return lax.all_to_all(copies, axis, dim, dim, tiled=True)  26.8 us
    all_gather x1, blocking collectives, local(): tkey_piece = lax.all_gather(text_key, 'row', axis=0, tiled=True)  25.2 us
    all_gather x1, blocking collectives, local(): tvalue_piece = lax.all_gather(text_value, 'row', axis=0, tiled=True)  22.3 us
    dot_general x1, matrix products, local(): jnp.einsum('sihd,kihd->ihsk', query, key_piece, preferred_element_type=jn...  21.7 us
    reduce_sum x1, other arithmetic, local(): jnp.sum(prob_img, axis=-1)  20.8 us
  transfers between devices with their start and end apart: 6, of which 5 were waited for; matrix products, arithmetic and copies ran while one was open for 12% of the time, Pallas kernels for 0%

profile of v1, /device:TPU:1, one launch (start us, length us, event | category | flops | bytes accessed | tf_op | source)
XLA Modules:
  0.0 487.8 jit_solution(7789156698399843077)
XLA Ops:
  6.5 3.6 pad_maximum_fusion
  10.1 0.5 broadcast.277
  10.6 4.9 %reduce.32 = bf16[512,2432]{1,0:T(8,128)(2,1)} reduce(bf16[512,1,2432]{2,0,1:T(8,128)(2,1)} %pad_maximum_fusion, bf16[]{:T(256)} %broadcast.277), dimensions={1}, to_apply=%copy.32.reduce_sub_computation | reduce | bytes 4980738 | tf_op jit(solution)/shard_map/concatenate | solution.py:10
  15.6 4.2 reshape.515
  19.8 6.0 %all-to-all-start = ((bf16[4,2,155648]{2,1,0:T(2,128)(2,1)}), bf16[4,2,155648]{2,1,0:T(2,128)(2,1)}, u32[]{:S(2)}, u32[]{:S(2)}) async-start(bf16[4,2,155648]{2,1,0:T(2,128)(2,1)} %reshape.515), calls=%async_computation | async-start | bytes 4980736 | tf_op jit(solution)/shard_map/all_to_all | solution.py:11
  26.4 2.2 fusion.77
  28.8 0.2 slice_reduce_fusion.1
  29.0 26.8 %all-to-all-done = bf16[4,2,155648]{2,1,0:T(2,128)(2,1)} async-done(((bf16[4,2,155648]{2,1,0:T(2,128)(2,1)}), bf16[4,2,155648]{2,1,0:T(2,128)(2,1)}, u32[]{:S(2)}, u32[]{:S(2)}) %all-to-all-start) | async-done | bytes 2490400 | tf_op jit(solution)/shard_map/all_to_all | solution.py:11
  55.7 5.4 %reshape.516 = bf16[512,1,2432]{2,1,0:T(2,128)(2,1)} reshape(bf16[4,2,155648]{2,1,0:T(2,128)(2,1)} %all-to-all-done) | data formatting | bytes 4980736
  61.1 2.9 convert_reduce_fusion
  64.0 1.0 copy-done.1
  65.0 0.8 fusion.8
  65.8 6.1 %fusion.39 = f32[3,512,1,384]{1,3,0,2:T(8,128)S(1)} fusion(bf16[2432,3,384]{2,0,1:T(8,128)(2,1)} %param.19, f32[2432]{0:T(1024)S(1)} %get-tuple-element.8, f32[2432]{0:T(1024)S(1)} %get-tuple-element.9, f32[512]{0:T(512)S(1)} %add_rsqrt_fusion.3, f32[512]{0:T(512)S(1)} %broadcast_multiply_fusion, bf16[512,1,2432]{2,1,0:T(2,128)(2,1)S(1)} %copy-done.1), kind=kOutput, calls=%fused_computation.46 | convolution fusion | flops 2876375040 | bytes 10476544 | tf_op jit(solution)/shard_map/sid,dce->csie/dot_general | solution.py:55
  71.9 1.4 copy-done.4
  73.3 1.6 slice_multiply_fusion.2
  74.9 1.2 reduce_sum.102
  76.3 2.1 fusion.64
  78.6 0.2 fusion.67
  78.8 2.7 fusion.56
  82.0 25.2 %all_gather.19 = bf16[160,1,384]{2,1,0:T(2,128)(2,1)S(1)} all-gather(bf16[20,1,384]{2,1,0:T(2,128)(2,1)S(1)} %copy.36), channel_id=1, replica_groups=mesh['item'=4,'row'=8,'col'=4] {'row'}, dimensions={0}, use_global_device_ids=true | all-gather | bytes 138240 | tf_op jit(solution)/shard_map/all_gather | solution.py:87
  107.2 0.2 copy.37
  108.1 0.6 dynamic-slice
  109.2 0.2 dynamic-update-slice
  109.5 16.3 %all-reduce = bf16[160]{0:T(256)(128)(2,1)S(1)} all-reduce(bf16[160]{0:T(256)(128)(2,1)S(1)} %dynamic-update-slice), channel_id=1, replica_groups=mesh['item'=4,'row'=8,'col'=4] {'row'}, use_global_device_ids=true, to_apply=%add | all-reduce | flops 160 | bytes 640
  125.8 22.3 %all-gather.1 = bf16[1,160,1,384]{3,2,0,1:T(2,128)(2,1)S(1)} all-gather(bf16[1,20,1,384]{3,2,0,1:T(2,128)(2,1)S(1)} %copy.38), channel_id=3, replica_groups=mesh['item'=4,'row'=8,'col'=4] {'row'}, dimensions={1}, use_global_device_ids=true | all-gather | bytes 138240 | tf_op jit(solution)/shard_map/all_gather | solution.py:88
  148.1 0.9 copy.39
  149.0 1.9 slice.74
  150.9 1.2 reduce_sum.101
  152.2 0.2 reduce-scatter.3.cloned.1.call-start
  152.4 2.9 fusion.38
  155.3 21.7 %multiply_reduce_fusion = (f32[6,512]{1,0:T(8,128)S(1)}, f32[6,512,4096]{2,1,0:T(8,128)}) fusion(bf16[4096,6,64]{0,2,1:T(8,128)(2,1)} %bitcast.91, f32[512,6,64]{0,2,1:T(8,128)} %bitcast.90, f32[64]{0:T(128)S(1)} %copy-done.9, f32[512,6]{0,1:T(8,128)S(1)} %add_rsqrt_fusion.1), kind=kOutput, calls=%fused_computation.1 | convolution fusion | flops 1636365312 | bytes 54288640 | tf_op jit(solution)/shard_map/sihd,kihd->ihsk/dot_general | solution.py:97
  177.0 2.0 fusion.42
  179.0 20.8 %fusion = f32[6,512]{1,0:T(8,128)S(1)} fusion(f32[6,512,4096]{2,1,0:T(8,128)} %get-tuple-element.19, f32[6,512]{1,0:T(8,128)S(1)} %get-tuple-element.14), kind=kLoop, calls=%fused_computation.2 | loop fusion | flops 37745664 | bytes 50356224 | tf_op jit(solution)/shard_map/reduce_sum | solution.py:109
  199.8 4.6 all-gather.9.cloned.1.call-done
  204.4 19.8 %fusion.47 = f32[6,512,64]{1,2,0:T(8,128)S(1)} fusion(bf16[4096,6,64]{0,2,1:T(8,128)(2,1)} %bitcast.95, f32[6,512,4096]{2,1,0:T(8,128)} %get-tuple-element.19, f32[6,512]{1,0:T(8,128)S(1)} %get-tuple-element.14, f32[6,512]{1,0:T(8,128)S(1)} %get-tuple-element.13), kind=kOutput, calls=%fused_computation.53 | convolution fusion | flops 1648558080 | bytes 54288384 | tf_op jit(solution)/shard_map/ihsk,kihd->ihsd/dot_general | solution.py:111
  224.3 0.6 fusion.50
  225.0 0.8 copy-done.5
  225.8 3.0 fusion.20
  228.9 39.8 %reduce-scatter.3.cloned.1.call-done = bf16[128,1,2432]{2,0,1:T(8,128)(2,1)} async-done(((bf16[512,1,2432]{2,0,1:T(8,128)(2,1)}), bf16[128,1,2432]{2,0,1:T(8,128)(2,1)}) %reduce-scatter.3.cloned.1.call-update) | async-done | bytes 622608 | tf_op jit(solution)/shard_map/reduce_scatter | solution.py:127
  268.7 1.6 convert_reduce_fusion.1
  270.3 0.3 fusion.51
  270.6 0.5 copy-done.2
  271.1 1.3 fusion.54
  272.4 0.3 reduce-scatter.5.cloned.1.call-start
  272.7 79.7 %all-gather.11.cloned.1.call-done = bf16[2048,1,2432]{2,0,1:T(8,128)(2,1)} async-done(((bf16[128,1,2432]{2,0,1:T(8,128)(2,1)}), bf16[2048,1,2432]{2,0,1:T(8,128)(2,1)}) %all-gather.11.cloned.1.call-update) | async-done | bytes 9961488 | tf_op jit(solution)/shard_map/all_gather | solution.py:142
  352.3 20.5 %convolution_convert_fusion = bf16[2048,2432]{1,0:T(8,128)(2,1)} fusion(bf16[608,2432]{1,0:T(8,128)(2,1)S(1)} %copy-done, bf16[2432,608]{0,1:T(8,128)(2,1)} %param.24, bf16[2048,1,2432]{2,0,1:T(8,128)(2,1)} %all-gather.11.cloned.1.call-done), kind=kOutput, calls=%fused_computation.5 | convolution fusion | flops 12129337344 | bytes 25837568 | tf_op jit(solution)/shard_map/dot_general | solution.py:150
  372.9 106.1 %reduce-scatter.5.cloned.1.call-done = bf16[128,2432]{1,0:T(8,128)(2,1)} async-done(((bf16[2048,2432]{1,0:T(8,128)(2,1)}), bf16[128,2432]{1,0:T(8,128)(2,1)}) %reduce-scatter.5.cloned.1.call-update) | async-done | bytes 622608 | tf_op jit(solution)/shard_map/reduce_scatter | solution.py:149
  479.0 2.3 fusion.55
  (58 shorter events, 1.1 us)
Async XLA Ops:
  6.5 345.8 %copy-start = (bf16[608,2432]{1,0:T(8,128)(2,1)S(1)}, bf16[608,2432]{1,0:T(8,128)(2,1)}, u32[]{:S(2)}) copy-start(bf16[608,2432]{1,0:T(8,128)(2,1)} %param.25) | copy-start | bytes 8871940
  19.8 8.9 %copy-start.10 = (f32[64]{0:T(128)S(1)}, f32[64]{0:T(128)}, u32[]{:S(2)}) copy-start(f32[64]{0:T(128)} %param.22) | copy-start | bytes 772
  19.8 9.0 %copy-start.8 = (f32[1,6,2432]{2,0,1:T(1,128)S(1)}, f32[1,6,2432]{2,0,1:T(1,128)}, u32[]{:S(2)}) copy-start(f32[1,6,2432]{2,0,1:T(1,128)} %param.18) | copy-start | bytes 175108
  19.8 36.0 %all-to-all-start = ((bf16[4,2,155648]{2,1,0:T(2,128)(2,1)}), bf16[4,2,155648]{2,1,0:T(2,128)(2,1)}, u32[]{:S(2)}, u32[]{:S(2)}) async-start(bf16[4,2,155648]{2,1,0:T(2,128)(2,1)} %reshape.515), calls=%async_computation | async-start | bytes 4980736 | tf_op jit(solution)/shard_map/all_to_all | solution.py:11
  25.8 129.6 %all-gather.7.cloned.1.call-start = ((), (), s32[]{:S(2)}) async-start(), calls=%async_computation.3 | async-start | bytes 3538944 | tf_op jit(solution)/shard_map/all_gather | solution.py:85
  61.1 3.9 copy-start.1
  71.9 1.4 copy-start.4
  74.9 3.5 copy-start.6
  78.4 29.7 %copy-start.11 = (u32[128]{0:T(128)S(1)}, u32[128]{0:T(128)}, u32[]{:S(2)}) copy-start(u32[128]{0:T(128)} %constant.56) | copy-start | bytes 1540
  78.4 126.0 %all-gather.9.cloned.1.call-start = ((), (), s32[]{:S(2)}) async-start(), calls=%async_computation.6 | async-start | bytes 3538944 | tf_op jit(solution)/shard_map/all_gather | solution.py:86
  81.5 70.9 %copy-start.9 = (f32[64]{0:T(128)S(1)}, f32[64]{0:T(128)}, u32[]{:S(2)}) copy-start(f32[64]{0:T(128)} %param.21) | copy-start | bytes 772
  152.2 116.5 %reduce-scatter.3.cloned.1.call-start = ((), (), s32[]{:S(2)}) async-start(), calls=%async_computation.4 | async-start | bytes 3112960 | tf_op jit(solution)/shard_map/reduce_scatter | solution.py:127
  204.4 19.9 %copy-start.3 = (f32[6,512,160]{1,2,0:T(8,128)S(1)}, f32[6,512,160]{1,2,0:T(8,128)}, u32[]{:S(2)}) copy-start(f32[6,512,160]{1,2,0:T(8,128)} %get-tuple-element.21) | copy-start | bytes 5898244
  204.4 19.9 %copy-start.7 = (bf16[1,160,1,384]{1,3,2,0:T(8,128)(2,1)S(1)}, bf16[1,160,1,384]{1,3,2,0:T(8,128)(2,1)}, u32[]{:S(2)}) copy-start(bf16[1,160,1,384]{1,3,2,0:T(8,128)(2,1)} %copy.39) | copy-start | bytes 368644
  224.3 1.5 copy-start.5
  228.8 123.5 %all-gather.11.cloned.1.call-start = ((), (), s32[]{:S(2)}) async-start(), calls=%async_computation.7 | async-start | bytes 10584064 | tf_op jit(solution)/shard_map/all_gather | solution.py:142
  270.3 0.8 copy-start.2
  272.4 206.6 %reduce-scatter.5.cloned.1.call-start = ((), (), s32[]{:S(2)}) async-start(), calls=%async_computation.5 | async-start | bytes 10584064 | tf_op jit(solution)/shard_map/reduce_scatter | solution.py:149
Sparse Core Ops, SparseCore 0:
  78.5 45.3 all-gather.6
  152.3 52.0 all-gather.8
  228.9 39.7 reduce-scatter.2
  272.5 79.7 all-gather.10
  373.0 105.9 reduce-scatter.4
